TPU v7x, 128 devices: a whole 4x4x4 slice. The times are simulated.
128 devices in a mesh: ctx: 16 (over z, y), head: 8 (over x, core).
Axes of the slice: x: 4, y: 4, z: 4, core: 2. Of those that a mesh axis runs over, the one named last changes fastest.
Arguments:
- queries: bfloat16 [32768, 8192], P(('ctx', 'head')), may hold values from -150 to 150
- key_states: bfloat16 [32768, 1024], P(('ctx', 'head')), may hold values from -10 to 10
- value_states: bfloat16 [32768, 1024], P(('ctx', 'head')), may hold values from -6 to 6
- page_ids: int32 [256], replicated, may hold values from 0 to 63, never falling along the last dimension, each value on 1 to 8 neighbouring positions
- ref_group: int32 [256, 4], replicated, may hold values from 0 to 15, all different within a row; in each aligned block of 16 rows (0 to 15, 16 to 31, ...) at most 4 rows name the same one
- ref_slot: int32 [256, 4], replicated, may hold values from 0 to 15
Outputs:
- attended: bfloat16 [32768, 8192], P(('ctx', 'head'))
Inputs may be any that keep to these rules, and one draw needn't show every extreme that they name: `page_ids`: ids never fall; every page has 1 to 8 blocks and one has exactly 8. `ref_group`: a row's 4 values differ; the rows of the 16 blocks of one ctx group name every ctx group exactly 4 times.
All inputs are finite; a program needn't handle non-finite values.
Results may differ from a plain program's by a relative error of at most 0.0042.
Values may be sent and summed in bfloat16 or wider, within the bound.
No kernel may reach another device: no remote copies, remote signals or barrier semaphores. Data moves between devices by JAX's collectives and lax.ppermute only.
A program may use at most 128 MiB of HBM per device.

v0:
```python
import math
import jax
import jax.numpy as jnp
from jax import lax
from jax.sharding import PartitionSpec as P

HD = 128
BLOCK = 128
MAXPAGE = 8


def from_behind(block, axis, distance):
    devices = range(lax.axis_size(axis))
    route = [(i - distance, i) for i in devices if i - distance in devices]
    return lax.ppermute(block, axis, route)


def page_starts(page_ids):
    block_count = page_ids.shape[0]
    position = jnp.arange(block_count, dtype=jnp.int32)
    is_fresh = jnp.concatenate([jnp.ones((1,), dtype=jnp.bool_), page_ids[1:] != page_ids[:-1]])
    return lax.cummax(jnp.where(is_fresh, position, jnp.zeros_like(position)), axis=0)


def allowed_mask(global_block, padded_pages, starts, ref_row, block_size, window):
    nearby = lax.dynamic_slice_in_dim(padded_pages, global_block, window, 0)
    own_page = nearby[window - 1]
    inside = nearby == own_page
    offsets = jnp.arange(window)
    is_last = offsets == window - 1
    rows_at = jnp.arange(block_size)
    causal = rows_at[None, :] <= rows_at[:, None]
    window_ok = inside[None, :, None] & (
        jnp.logical_not(is_last)[None, :, None] | causal[:, None, :]
    )
    window_ok = window_ok.reshape(block_size, window * block_size)
    start_here = lax.dynamic_index_in_dim(starts, global_block, 0, keepdims=False)
    ref_ok = ref_row < start_here
    ref_ok = jnp.broadcast_to(ref_ok[None, :, None], (block_size, ref_row.shape[0], block_size))
    return jnp.concatenate([window_ok, ref_ok.reshape(block_size, -1)], axis=1)


def attend(query_block, key_set, value_set, allowed):
    score_scale = 1.0 / math.sqrt(query_block.shape[-1])
    scores = (
        jnp.einsum("tgqd,sgd->gqts", query_block, key_set, preferred_element_type=jnp.float32)
        * score_scale
    )
    scores = jnp.where(allowed, scores, -1e30)
    row_max = jnp.max(scores, axis=-1, keepdims=True)
    exp_scores = jnp.where(allowed, jnp.exp(scores - row_max), 0.0)
    totals = jnp.sum(exp_scores, axis=-1)
    weights = exp_scores.astype(jnp.bfloat16)
    mixture = jnp.einsum("gqts,sgd->tgqd", weights, value_set, preferred_element_type=jnp.float32)
    return (mixture / jnp.transpose(totals, (2, 0, 1))[..., None]).astype(jnp.bfloat16)


def shards(queries, key_states, value_states, page_ids, ref_group, ref_slot):
    head_queries, head_keys, head_values = (
        lax.all_to_all(queries, "head", split_axis=1, concat_axis=0, tiled=True),
        lax.all_to_all(key_states, "head", split_axis=1, concat_axis=0, tiled=True),
        lax.all_to_all(value_states, "head", split_axis=1, concat_axis=0, tiled=True),
    )
    group_tokens = head_keys.shape[0]
    key_width = head_keys.shape[1]
    local_heads = key_width // HD
    blocks = group_tokens // BLOCK
    reach = MAXPAGE - 1
    refs_count = ref_group.shape[1]
    key_blocks = head_keys.reshape(blocks, BLOCK, key_width)
    value_blocks = head_values.reshape(blocks, BLOCK, key_width)
    tail_keys, tail_values = from_behind(
        (key_blocks[blocks - reach :], value_blocks[blocks - reach :]), "ctx", 1
    )
    near_keys = jnp.concatenate([tail_keys, key_blocks])
    near_values = jnp.concatenate([tail_values, value_blocks])
    ctx_group = lax.axis_index("ctx")
    first_block = ctx_group * blocks
    own_groups = lax.dynamic_slice_in_dim(ref_group, first_block, blocks, 0)
    own_slots = lax.dynamic_slice_in_dim(ref_slot, first_block, blocks, 0)
    own_rows = own_groups * blocks + own_slots
    whole_keys, whole_values = (
        lax.all_gather(key_blocks, "ctx", axis=0, tiled=True),
        lax.all_gather(value_blocks, "ctx", axis=0, tiled=True),
    )
    flat_rows = own_rows.reshape(-1)
    far_keys = jnp.take(whole_keys, flat_rows, axis=0).reshape(blocks, refs_count, BLOCK, key_width)
    far_values = jnp.take(whole_values, flat_rows, axis=0).reshape(
        blocks, refs_count, BLOCK, key_width
    )
    padded_pages = jnp.concatenate([jnp.full((reach,), -1, dtype=jnp.int32), page_ids])
    starts = page_starts(page_ids)
    group_size = head_queries.shape[1] // key_width
    query_blocks = head_queries.reshape(blocks, BLOCK, local_heads, group_size, HD)

    def one_block(local_block):
        global_block = first_block + local_block
        ref_row = lax.dynamic_index_in_dim(own_rows, local_block, 0, keepdims=False)
        key_set = jnp.concatenate(
            [
                lax.dynamic_slice_in_dim(near_keys, local_block, MAXPAGE, 0),
                lax.dynamic_index_in_dim(far_keys, local_block, 0, keepdims=False),
            ]
        )
        value_set = jnp.concatenate(
            [
                lax.dynamic_slice_in_dim(near_values, local_block, MAXPAGE, 0),
                lax.dynamic_index_in_dim(far_values, local_block, 0, keepdims=False),
            ]
        )
        allowed = allowed_mask(global_block, padded_pages, starts, ref_row, BLOCK, MAXPAGE)
        query_block = lax.dynamic_index_in_dim(query_blocks, local_block, 0, keepdims=False)
        return attend(
            query_block,
            key_set.reshape(-1, local_heads, HD),
            value_set.reshape(-1, local_heads, HD),
            allowed,
        )

    outputs = lax.map(one_block, jnp.arange(blocks, dtype=jnp.int32))
    merged = outputs.reshape(group_tokens, head_queries.shape[1])
    return lax.all_to_all(merged, "head", split_axis=0, concat_axis=1, tiled=True)


def solution(mesh):
    placed = (
        P(("ctx", "head"), None),
        P(("ctx", "head"), None),
        P(("ctx", "head"), None),
        P(),
        P(),
        P(),
    )
    return jax.shard_map(
        shards, mesh=mesh, in_specs=placed, out_specs=P(("ctx", "head"), None), check_vma=False
    )
```

profile of v0, /device:TPU:1, one launch (start us, length us, event | category | flops | bytes accessed | tf_op | source)
XLA Modules:
  0.0 519.4 jit_solution(513064871498028624)
XLA Ops:
  7.7 15.0 %all_to_all.67 = bf16[256,8,128]{2,0,1:T(8,128)(2,1)} all-to-all(bf16[256,8,128]{2,0,1:T(8,128)(2,1)S(1)} %copy_bitcast_fusion.4), channel_id=1, replica_groups=mesh['ctx'=16,'head'=8] {'head'}, dimensions={1} | all-to-all | bytes 1048576 | tf_op jit(solution)/shard_map/all_to_all | solution.py:62
  23.9 13.4 %all_to_all.68 = bf16[256,8,128]{2,0,1:T(8,128)(2,1)} all-to-all(bf16[256,8,128]{2,0,1:T(8,128)(2,1)S(1)} %copy_bitcast_fusion.3), channel_id=1, replica_groups=mesh['ctx'=16,'head'=8] {'head'}, dimensions={1} | all-to-all | bytes 1048576 | tf_op jit(solution)/shard_map/all_to_all | solution.py:61
  37.4 4.8 copy.62
  42.2 5.6 %all-to-all-start.2 = ((bf16[256,8,1024]{2,0,1:T(8,128)(2,1)}), bf16[256,8,1024]{2,0,1:T(8,128)(2,1)}, u32[]{:S(2)}, u32[]{:S(2)}) async-start(bf16[256,8,1024]{2,0,1:T(8,128)(2,1)} %bitcast.164), calls=%async_computation.2 | async-start | bytes 8388608 | tf_op jit(solution)/shard_map/all_to_all | solution.py:60
  49.0 3.2 collective-permute-start
  52.3 3.2 collective-permute-start.1
  58.0 8.6 %collective-permute-done.1 = bf16[7,128,128]{2,1,0:T(8,128)(2,1)S(1)} collective-permute-done((bf16[7,128,128]{2,1,0:T(8,128)(2,1)S(1)}, bf16[7,128,128]{2,1,0:T(8,128)(2,1)S(1)}, u32[]{:S(2)}, u32[]{:S(2)}) %collective-permute-start.1) | collective-permute-done | bytes 229408 | tf_op jit(solution)/shard_map/ppermute | solution.py:15
  67.5 29.1 %all-to-all-done.2 = bf16[256,8,1024]{2,0,1:T(8,128)(2,1)} async-done(((bf16[256,8,1024]{2,0,1:T(8,128)(2,1)}), bf16[256,8,1024]{2,0,1:T(8,128)(2,1)}, u32[]{:S(2)}, u32[]{:S(2)}) %all-to-all-start.2) | async-done | bytes 4194336 | tf_op jit(solution)/shard_map/all_to_all | solution.py:60
  96.6 5.2 %copy.54 = bf16[256,8,8,128]{3,2,1,0:T(8,128)(2,1)} copy(bf16[256,8,8,128]{3,1,2,0:T(8,128)(2,1)} %bitcast.50) | data formatting | bytes 8388608
  101.8 4.3 gather_fusion
  106.1 66.7 %all-gather.5.cloned.1.call-done = bf16[256,128,128]{2,1,0:T(8,128)(2,1)} async-done(((bf16[16,128,128]{2,1,0:T(8,128)(2,1)}), bf16[256,128,128]{2,1,0:T(8,128)(2,1)}) %all-gather.5.cloned.1.call-update) | async-done | bytes 8388624 | tf_op jit(solution)/shard_map/all_gather | solution.py:83
  172.9 5.6 %gather_fusion.1 = bf16[64,128,128]{2,1,0:T(8,128)(2,1)} fusion(bf16[256,128,128]{2,1,0:T(8,128)(2,1)} %all-gather.5.cloned.1.call-done, s32[1024]{0:T(1024)S(1)} %pad_clamp_fusion), kind=kCustom, calls=%fused_computation.1.clone | custom fusion | bytes 4194560 | tf_op jit(solution)/shard_map/jit(_take)/gather | solution.py:87
  178.4 4.0 broadcast_select_fusion
  182.4 256.0 %while.10 = (s32[]{:T(128)}, bf16[16,128,1,8,128]{4,3,1,0,2:T(8,128)(2,1)}, s32[16]{0:T(128)S(1)}, bf16[23,128,128]{2,1,0:T(8,128)(2,1)}, bf16[16,4,128,128]{3,2...) while((s32[]{:T(128)}, ...), condition=%wide.region_5.7_spmd, body=%wide.region_2.6_spmd.sunk | while | flops 826882048 | bytes 26014728 | solution.py:120
  195.8 1.7 fusion.42
  227.8 1.7 fusion.42
  243.8 1.7 fusion.42
  259.8 1.7 fusion.42
  275.8 1.7 fusion.42
  291.8 1.7 fusion.42
  307.8 1.7 fusion.42
  323.8 1.7 fusion.42
  339.8 1.7 fusion.42
  355.8 1.7 fusion.42
  371.8 1.7 fusion.42
  387.8 1.7 fusion.42
  403.8 1.7 fusion.42
  419.8 1.7 fusion.42
  438.4 7.3 %all_to_all.59 = bf16[8,256,1024]{2,1,0:T(8,128)(2,1)} reshape(bf16[16,128,1,8,128]{4,3,1,0,2:T(8,128)(2,1)} %get-tuple-element.68) | data formatting | bytes 8388608 | tf_op jit(solution)/shard_map/all_to_all | solution.py:122
  445.8 54.0 %all_to_all.69 = bf16[8,256,1024]{2,1,0:T(8,128)(2,1)} all-to-all(bf16[8,256,1024]{2,1,0:T(8,128)(2,1)} %all_to_all.59), channel_id=1, replica_groups=mesh['ctx'=16,'head'=8] {'head'}, dimensions={0} | all-to-all | bytes 8388608 | tf_op jit(solution)/shard_map/all_to_all | solution.py:122
  499.7 6.5 %copy.41 = bf16[256,8,1024]{0,2,1:T(8,128)(2,1)} copy(bf16[256,8,1024]{2,0,1:T(8,128)(2,1)} %bitcast.165) | data formatting | bytes 8388608 | tf_op jit(solution)/shard_map/all_to_all | solution.py:122
  506.2 6.4 %copy.42 = bf16[256,8192]{1,0:T(8,128)(2,1)} copy(bf16[256,8192]{0,1:T(8,128)(2,1)} %bitcast.166) | data formatting | bytes 8388608 | tf_op jit(solution)/shard_map/all_to_all | solution.py:122
  (398 shorter events, 177.3 us)
Async XLA Ops:
  6.5 1.0 copy-start
  6.5 95.3 %all-gather.3.cloned.1.call-start = ((), (), s32[]{:S(2)}) async-start(), calls=%async_computation.4 | async-start | bytes 8912896 | tf_op jit(solution)/shard_map/all_gather | solution.py:84
  22.7 150.2 %all-gather.5.cloned.1.call-start = ((), (), s32[]{:S(2)}) async-start(), calls=%async_computation.5 | async-start | bytes 8912896 | tf_op jit(solution)/shard_map/all_gather | solution.py:83
  42.1 5.6 %copy-start.5 = (s32[256,4]{0,1:T(4,128)S(1)}, s32[256,4]{0,1:T(4,128)}, u32[]{:S(2)}) copy-start(s32[256,4]{0,1:T(4,128)} %param.15) | copy-start | bytes 12292
  42.1 5.6 %copy-start.6 = (s32[256,4]{0,1:T(4,128)S(1)}, s32[256,4]{0,1:T(4,128)}, u32[]{:S(2)}) copy-start(s32[256,4]{0,1:T(4,128)} %param.14) | copy-start | bytes 12292
  42.2 6.0 %copy-start.4 = (s32[256]{0:T(256)S(1)}, s32[256]{0:T(256)}, u32[]{:S(2)}) copy-start(s32[256]{0:T(256)} %param.13) | copy-start | bytes 3076
  42.2 6.8 %copy-start.2 = (bf16[256,8,128]{2,0,1:T(8,128)(2,1)S(1)}, bf16[256,8,128]{2,0,1:T(8,128)(2,1)}, u32[]{:S(2)}) copy-start(bf16[256,8,128]{2,0,1:T(8,128)(2,1)} %all_to_all.67) | copy-start | bytes 1572868
  42.2 10.1 %copy-start.3 = (bf16[256,8,128]{2,0,1:T(8,128)(2,1)S(1)}, bf16[256,8,128]{2,0,1:T(8,128)(2,1)}, u32[]{:S(2)}) copy-start(bf16[256,8,128]{2,0,1:T(8,128)(2,1)} %all_to_all.68) | copy-start | bytes 1572868
  42.2 54.4 %all-to-all-start.2 = ((bf16[256,8,1024]{2,0,1:T(8,128)(2,1)}), bf16[256,8,1024]{2,0,1:T(8,128)(2,1)}, u32[]{:S(2)}, u32[]{:S(2)}) async-start(bf16[256,8,1024]{2,0,1:T(8,128)(2,1)} %bitcast.164), calls=%async_computation.2 | async-start | bytes 8388608 | tf_op jit(solution)/shard_map/all_to_all | solution.py:60
  49.0 8.0 %collective-permute-start = (bf16[7,128,128]{2,1,0:T(8,128)(2,1)S(1)}, bf16[7,128,128]{2,1,0:T(8,128)(2,1)S(1)}, u32[]{:S(2)}, u32[]{:S(2)}) collective-permute-start(bf16[7,128,128]{2,1,0:T(8,128)(2,1)S(1)} %slice.32), channel_id=1, source_target_pairs={{0,8},{8,16},{16,24},{24,32},{32,40},{40,48},{48,56},{56,64},{64,7... | collective-permute-start | bytes 688136 | tf_op jit(solution)/shard_map/ppermute | solution.py:15
  52.3 14.3 %collective-permute-start.1 = (bf16[7,128,128]{2,1,0:T(8,128)(2,1)S(1)}, bf16[7,128,128]{2,1,0:T(8,128)(2,1)S(1)}, u32[]{:S(2)}, u32[]{:S(2)}) collective-permute-start(bf16[7,128,128]{2,1,0:T(8,128)(2,1)S(1)} %slice.33), channel_id=1, source_target_pairs={{0,8},{8,16},{16,24},{24,32},{32,40},{40,48},{48,56},{56,64},{64,7... | collective-permute-start | bytes 688136 | tf_op jit(solution)/shard_map/ppermute | solution.py:15
  506.2 6.4 %copy-start.1 = (bf16[256,1024]{1,0:T(8,128)(2,1)S(1)}, bf16[256,1024]{1,0:T(8,128)(2,1)}, u32[]{:S(2)}) copy-start(bf16[256,1024]{1,0:T(8,128)(2,1)} %param.12) | copy-start | bytes 1572868
Sparse Core Ops, SparseCore 0:
  22.8 77.1 all-gather.2
  102.2 70.6 all-gather.4
where the time goes:
time: 523 us; the launch traced here: 519 us
  local copies, waits for them, and re-layouts  139 us (27%)
  waiting for transfers between devices  106 us (20%)
  blocking collectives  82.4 us (16%)
  loops' own time  62.4 us (12%)
  other arithmetic  61.2 us (12%)
  matrix products  43.3 us (8%)
  between operations  13.5 us (3%)
  starting transfers between devices  12.1 us (2%)
    all_gather x1, waiting for transfers between devices, shards(): lax.all_gather(key_blocks, 'ctx', axis=0, tiled=True)  66.7 us
    another operation x1, loops' own time, shards(): outputs = lax.map(one_block, jnp.arange(blocks, dtype=jnp.int32))  62.4 us
    all_to_all x1, blocking collectives, shards(): lax.all_to_all(merged, 'head', split_axis=0, concat_axis=1, tiled=True)  54 us
    all_to_all x1, waiting for transfers between devices, shards(): lax.all_to_all(queries, 'head', split_axis=1, concat_axis=0, tiled=True)  29.1 us
    dot_general x16, matrix products, attend(): jnp.einsum('gqts,sgd->tgqd', weights, value_set, preferred_element_type=j...  26.6 us
    reduce_sum x16, other arithmetic, attend(): totals = jnp.sum(exp_scores, axis=-1)  24.1 us
    all_to_all x3, local copies, waits for them, and re-layouts, shards(): lax.all_to_all(merged, 'head', split_axis=0, concat_axis=1, tiled=True)  20.2 us
    dynamic_slice x16, local copies, waits for them, and re-layouts, one_block(): lax.dynamic_slice_in_dim(near_keys, local_block, MAXPAGE, 0)  17.1 us
  transfers between devices with their start and end apart: 5, of which 4 were waited for; matrix products, arithmetic and copies ran while one was open for 4% of the time, Pallas kernels for 0%

commit v1 on v0

--- a/solution.py
+++ b/solution.py
@@ -79,8 +79,36 @@
     own_groups = lax.dynamic_slice_in_dim(ref_group, first_block, blocks, 0)
     own_slots = lax.dynamic_slice_in_dim(ref_slot, first_block, blocks, 0)
     own_rows = own_groups * blocks + own_slots
+
+    def turns_trace(vector):
+        q_next, g_now, t1 = (jax.lax.axis_size("ctx"), jax.lax.axis_index("ctx"), vector.shape[0])
+        pool = []
+        for tick, m in enumerate(vector.shape):
+            pool.append(m * q_next if tick == 0 else m)
+        w_next = now = vector
+        front = lax.dynamic_update_slice_in_dim(
+            jnp.zeros(pool, vector.dtype), vector, g_now * t1, axis=0
+        )
+        for dev_i in range(1, q_next // 2 + 1):
+            crops = []
+            for tick in range(q_next):
+                crops.append((tick, (tick + 1) % q_next))
+            w_next = jax.lax.ppermute(w_next, "ctx", crops)
+            front = lax.dynamic_update_slice_in_dim(
+                front, w_next, (g_now - dev_i) % q_next * t1, axis=0
+            )
+            if 2 * dev_i < q_next:
+                seen = []
+                for tick in range(q_next):
+                    seen.append((tick, (tick - 1) % q_next))
+                now = jax.lax.ppermute(now, "ctx", perm=seen)
+                front = lax.dynamic_update_slice_in_dim(
+                    front, now, (g_now + dev_i) % q_next * t1, axis=0
+                )
+        return front
+
     whole_keys, whole_values = (
-        lax.all_gather(key_blocks, "ctx", axis=0, tiled=True),
+        turns_trace(key_blocks),
         lax.all_gather(value_blocks, "ctx", axis=0, tiled=True),
     )
     flat_rows = own_rows.reshape(-1)

time: 523 us -> 554 us (1.059)
  starting transfers between devices: 12.1 us -> 46.7 us
  waiting for transfers between devices: 106 us -> 71.7 us
  local copies, waits for them, and re-layouts: 139 us -> 163 us
    ppermute x0 -> x15, waiting for transfers between devices: none -> 68.2 us  [the longest x7 35.4 us: turns_trace(): now = jax.lax.ppermute(now, 'ctx', perm=seen)]
    all_gather x1 -> x0, waiting for transfers between devices: 66.7 us -> none  [shards(): lax.all_gather(key_blocks, 'ctx', axis=0, tiled=True)]
    ppermute x0 -> x15, starting transfers between devices: none -> 38.5 us  [the longest x7 33 us: turns_trace(): now = jax.lax.ppermute(now, 'ctx', perm=seen)]
    all_to_all x1, waiting for transfers between devices: 29.1 us -> 0.01 us  [shards(): lax.all_to_all(queries, 'head', split_axis=1, concat_axis=0, tiled=True)]
    dynamic_update_slice x0 -> x16, local copies, waits for them, and re-layouts: none -> 17.8 us  [the longest x8 8.85 us: turns_trace(): lax.dynamic_update_slice_in_dim(front, w_next, (g_now - dev_i) % q_next *...]
    ppermute x2, waiting for transfers between devices: 10 us -> 3.48 us  [from_behind(): return lax.ppermute(block, axis, route)]
  transfers between devices with their start and end apart: 5 -> 19, of which waited for: 4 -> 12; matrix products, arithmetic and copies ran while one was open for 4% -> 7% of each run, Pallas kernels for 0% -> 0%
where the time goes in v1:
time: 554 us; the launch traced here: 551 us
  local copies, waits for them, and re-layouts  163 us (29%)
  blocking collectives  85.4 us (15%)
  waiting for transfers between devices  71.7 us (13%)
  other arithmetic  64.7 us (12%)
  loops' own time  62.2 us (11%)
  starting transfers between devices  46.7 us (8%)
  matrix products  43.4 us (8%)
  between operations  13.5 us (2%)
    another operation x1, loops' own time, shards(): outputs = lax.map(one_block, jnp.arange(blocks, dtype=jnp.int32))  62.2 us
    all_to_all x1, blocking collectives, shards(): lax.all_to_all(merged, 'head', split_axis=0, concat_axis=1, tiled=True)  57.6 us
    ppermute x7, waiting for transfers between devices, turns_trace(): now = jax.lax.ppermute(now, 'ctx', perm=seen)  35.4 us
    ppermute x7, starting transfers between devices, turns_trace(): now = jax.lax.ppermute(now, 'ctx', perm=seen)  33 us
    ppermute x8, waiting for transfers between devices, turns_trace(): w_next = jax.lax.ppermute(w_next, 'ctx', crops)  32.8 us
    dot_general x16, matrix products, attend(): jnp.einsum('gqts,sgd->tgqd', weights, value_set, preferred_element_type=j...  26.7 us
    reduce_sum x16, other arithmetic, attend(): totals = jnp.sum(exp_scores, axis=-1)  24.3 us
    all_to_all x3, local copies, waits for them, and re-layouts, shards(): lax.all_to_all(merged, 'head', split_axis=0, concat_axis=1, tiled=True)  20.2 us
  transfers between devices with their start and end apart: 19, of which 12 were waited for; matrix products, arithmetic and copies ran while one was open for 7% of the time, Pallas kernels for 0%

profile of v1, /device:TPU:1, one launch (start us, length us, event | category | flops | bytes accessed | tf_op | source)
XLA Modules:
  0.0 550.8 jit_solution(9582360999959723014)
XLA Ops:
  7.7 15.0 %all_to_all.67 = bf16[256,8,128]{2,0,1:T(8,128)(2,1)} all-to-all(bf16[256,8,128]{2,0,1:T(8,128)(2,1)S(1)} %copy_bitcast_fusion.4), channel_id=1, replica_groups=mesh['ctx'=16,'head'=8] {'head'}, dimensions={1} | all-to-all | bytes 1048576 | tf_op jit(solution)/shard_map/all_to_all | solution.py:62
  23.9 12.8 %all_to_all.68 = bf16[256,8,128]{2,0,1:T(8,128)(2,1)S(1)} all-to-all(bf16[256,8,128]{2,0,1:T(8,128)(2,1)S(1)} %copy_bitcast_fusion.3), channel_id=1, replica_groups=mesh['ctx'=16,'head'=8] {'head'}, dimensions={1} | all-to-all | bytes 1048576 | tf_op jit(solution)/shard_map/all_to_all | solution.py:61
  37.9 5.0 collective-permute-start.3
  42.9 17.0 %collective-permute-done.2 = bf16[16,128,128]{2,1,0:T(8,128)(2,1)S(1)} collective-permute-done((bf16[16,128,128]{2,1,0:T(8,128)(2,1)S(1)}, bf16[16,128,128]{2,1,0:T(8,128)(2,1)S(1)}, u32[]{:S(2)}, u32[]{:S(2)}) %collective-permute-start.2) | collective-permute-done | bytes 524320 | tf_op jit(solution)/shard_map/ppermute | solution.py:96
  59.9 4.8 copy.62
  64.7 5.5 %all-to-all-start.2 = ((bf16[256,8,1024]{2,0,1:T(8,128)(2,1)}), bf16[256,8,1024]{2,0,1:T(8,128)(2,1)}, u32[]{:S(2)}, u32[]{:S(2)}) async-start(bf16[256,8,1024]{2,0,1:T(8,128)(2,1)} %bitcast.164), calls=%async_computation.2 | async-start | bytes 8388608 | tf_op jit(solution)/shard_map/all_to_all | solution.py:60
  70.2 5.1 collective-permute-start.5
  75.6 3.7 collective-permute-done.4
  79.3 18.9 %collective-permute-done.5 = bf16[16,128,128]{2,1,0:T(8,128)(2,1)S(1)} collective-permute-done((bf16[16,128,128]{2,1,0:T(8,128)(2,1)S(1)}, bf16[16,128,128]{2,1,0:T(8,128)(2,1)S(1)}, u32[]{:S(2)}, u32[]{:S(2)}) %collective-permute-start.5) | collective-permute-done | bytes 524320 | tf_op jit(solution)/shard_map/ppermute | solution.py:104
  98.2 5.5 %collective-permute-start.7 = (bf16[16,128,128]{2,1,0:T(8,128)(2,1)S(1)}, bf16[16,128,128]{2,1,0:T(8,128)(2,1)}, u32[]{:S(2)}, u32[]{:S(2)}) collective-permute-start(bf16[16,128,128]{2,1,0:T(8,128)(2,1)S(1)} %collective-permute-done.5), channel_id=1, source_target_pairs={{0,120},{8,0},{16,8},{24,16},{32,24},{40,32},{48,40},{56,48},{64,5... | collective-permute-start | bytes 1572872 | tf_op jit(solution)/shard_map/ppermute | solution.py:104
  104.4 2.1 collective-permute-done.6
  106.7 16.5 %collective-permute-done.7 = bf16[16,128,128]{2,1,0:T(8,128)(2,1)} collective-permute-done((bf16[16,128,128]{2,1,0:T(8,128)(2,1)S(1)}, bf16[16,128,128]{2,1,0:T(8,128)(2,1)}, u32[]{:S(2)}, u32[]{:S(2)}) %collective-permute-start.7) | collective-permute-done | bytes 524320 | tf_op jit(solution)/shard_map/ppermute | solution.py:104
  123.2 4.9 collective-permute-start.9
  128.2 3.5 collective-permute-done.8
  134.4 5.3 broadcast_in_dim.53
  140.7 4.7 collective-permute-start.11
  146.6 2.0 collective-permute-start.12
  148.6 2.6 collective-permute-done
  154.7 5.3 collective-permute-start.13
  162.4 2.2 collective-permute-start.14
  166.5 1.9 constant_dynamic-update-slice_fusion.10
  172.2 2.6 collective-permute-start.15
  179.0 5.3 copy.54
  186.0 3.7 collective-permute-done.16
  190.7 4.3 gather_fusion.1
  195.0 5.6 %gather_fusion = bf16[64,128,128]{2,1,0:T(8,128)(2,1)} fusion(bf16[256,128,128]{2,1,0:T(8,128)(2,1)} %all-gather.2.cloned.1.call-done, s32[1024]{0:T(1024)S(1)} %pad_clamp_fusion), kind=kCustom, calls=%fused_computation.clone | custom fusion | bytes 4194560 | tf_op jit(solution)/shard_map/jit(_take)/gather | solution.py:116
  200.6 4.0 broadcast_select_fusion
  204.6 261.5 %while.10 = (s32[]{:T(128)}, bf16[16,128,1,8,128]{4,3,1,0,2:T(8,128)(2,1)}, s32[16]{0:T(128)S(1)}, bf16[23,128,128]{2,1,0:T(8,128)(2,1)}, bf16[16,4,128,128]{3,2...) while((s32[]{:T(128)}, ...), condition=%wide.region_5.7_spmd, body=%wide.region_2.6_spmd.sunk | while | flops 826882048 | bytes 26014728 | solution.py:148
  466.1 7.3 %all_to_all.59 = bf16[8,256,1024]{2,1,0:T(8,128)(2,1)} reshape(bf16[16,128,1,8,128]{4,3,1,0,2:T(8,128)(2,1)} %get-tuple-element.68) | data formatting | bytes 8388608 | tf_op jit(solution)/shard_map/all_to_all | solution.py:150
  473.4 57.6 %all_to_all.69 = bf16[8,256,1024]{2,1,0:T(8,128)(2,1)} all-to-all(bf16[8,256,1024]{2,1,0:T(8,128)(2,1)} %all_to_all.59), channel_id=1, replica_groups=mesh['ctx'=16,'head'=8] {'head'}, dimensions={0} | all-to-all | bytes 8388608 | tf_op jit(solution)/shard_map/all_to_all | solution.py:150
  531.1 6.6 %copy.41 = bf16[256,8,1024]{0,2,1:T(8,128)(2,1)} copy(bf16[256,8,1024]{2,0,1:T(8,128)(2,1)} %bitcast.165) | data formatting | bytes 8388608 | tf_op jit(solution)/shard_map/all_to_all | solution.py:150
  537.6 6.3 %copy.42 = bf16[256,8192]{1,0:T(8,128)(2,1)} copy(bf16[256,8192]{0,1:T(8,128)(2,1)} %bitcast.166) | data formatting | bytes 8388608 | tf_op jit(solution)/shard_map/all_to_all | solution.py:150
  (444 shorter events, 227.4 us)
Async XLA Ops:
  6.5 1.0 copy-start
  6.5 188.5 %all-gather.2.cloned.1.call-start = ((), (), s32[]{:S(2)}) async-start(), calls=%async_computation.4 | async-start | bytes 8912896 | tf_op jit(solution)/shard_map/all_gather | solution.py:112
  36.6 23.3 %collective-permute-start.2 = (bf16[16,128,128]{2,1,0:T(8,128)(2,1)S(1)}, bf16[16,128,128]{2,1,0:T(8,128)(2,1)S(1)}, u32[]{:S(2)}, u32[]{:S(2)}) collective-permute-start(bf16[16,128,128]{2,1,0:T(8,128)(2,1)S(1)} %bitcast.172), channel_id=1, source_target_pairs={{0,8},{8,16},{16,24},{24,32},{32,40},{40,48},{48,56},{56,64},{64,7... | collective-permute-start | bytes 1572872 | tf_op jit(solution)/shard_map/ppermute | solution.py:96
  37.9 32.3 %collective-permute-start.3 = (bf16[16,128,128]{2,1,0:T(8,128)(2,1)S(1)}, bf16[16,128,128]{2,1,0:T(8,128)(2,1)S(1)}, u32[]{:S(2)}, u32[]{:S(2)}) collective-permute-start(bf16[16,128,128]{2,1,0:T(8,128)(2,1)S(1)} %bitcast.173), channel_id=1, source_target_pairs={{0,120},{8,0},{16,8},{24,16},{32,24},{40,32},{48,40},{56,48},{64,5... | collective-permute-start | bytes 1572872 | tf_op jit(solution)/shard_map/ppermute | solution.py:104
  59.9 19.4 %collective-permute-start.4 = (bf16[16,128,128]{2,1,0:T(8,128)(2,1)S(1)}, bf16[16,128,128]{2,1,0:T(8,128)(2,1)S(1)}, u32[]{:S(2)}, u32[]{:S(2)}) collective-permute-start(bf16[16,128,128]{2,1,0:T(8,128)(2,1)S(1)} %collective-permute-done.2), channel_id=1, source_target_pairs={{0,8},{8,16},{16,24},{24,32},{32,40},{40,48},{48,56},{56,64},{64,7... | collective-permute-start | bytes 1572872 | tf_op jit(solution)/shard_map/ppermute | solution.py:96
  64.7 10.6 %copy-start.6 = (s32[256,4]{0,1:T(4,128)S(1)}, s32[256,4]{0,1:T(4,128)}, u32[]{:S(2)}) copy-start(s32[256,4]{0,1:T(4,128)} %param.15) | copy-start | bytes 12292
  64.7 10.6 %copy-start.7 = (s32[256,4]{0,1:T(4,128)S(1)}, s32[256,4]{0,1:T(4,128)}, u32[]{:S(2)}) copy-start(s32[256,4]{0,1:T(4,128)} %param.14) | copy-start | bytes 12292
  64.7 39.0 %copy-start.5 = (s32[256]{0:T(256)S(1)}, s32[256]{0:T(256)}, u32[]{:S(2)}) copy-start(s32[256]{0:T(256)} %param.13) | copy-start | bytes 3076
  64.7 68.4 %copy-start.2 = (bf16[256,8,128]{2,0,1:T(8,128)(2,1)S(1)}, bf16[256,8,128]{2,0,1:T(8,128)(2,1)}, u32[]{:S(2)}) copy-start(bf16[256,8,128]{2,0,1:T(8,128)(2,1)} %all_to_all.67) | copy-start | bytes 1572868
  64.7 114.3 %all-to-all-start.2 = ((bf16[256,8,1024]{2,0,1:T(8,128)(2,1)}), bf16[256,8,1024]{2,0,1:T(8,128)(2,1)}, u32[]{:S(2)}, u32[]{:S(2)}) async-start(bf16[256,8,1024]{2,0,1:T(8,128)(2,1)} %bitcast.164), calls=%async_computation.2 | async-start | bytes 8388608 | tf_op jit(solution)/shard_map/all_to_all | solution.py:60
  70.2 27.9 %collective-permute-start.5 = (bf16[16,128,128]{2,1,0:T(8,128)(2,1)S(1)}, bf16[16,128,128]{2,1,0:T(8,128)(2,1)S(1)}, u32[]{:S(2)}, u32[]{:S(2)}) collective-permute-start(bf16[16,128,128]{2,1,0:T(8,128)(2,1)S(1)} %collective-permute-done.3), channel_id=1, source_target_pairs={{0,120},{8,0},{16,8},{24,16},{32,24},{40,32},{48,40},{56,48},{64,5... | collective-permute-start | bytes 1572872 | tf_op jit(solution)/shard_map/ppermute | solution.py:104
  79.3 27.2 %collective-permute-start.6 = (bf16[16,128,128]{2,1,0:T(8,128)(2,1)S(1)}, bf16[16,128,128]{2,1,0:T(8,128)(2,1)}, u32[]{:S(2)}, u32[]{:S(2)}) collective-permute-start(bf16[16,128,128]{2,1,0:T(8,128)(2,1)S(1)} %collective-permute-done.4), channel_id=1, source_target_pairs={{0,8},{8,16},{16,24},{24,32},{32,40},{40,48},{48,56},{56,64},{64,7... | collective-permute-start | bytes 1572872 | tf_op jit(solution)/shard_map/ppermute | solution.py:96
  98.2 47.2 %copy-start.3 = (bf16[16,128,128]{2,1,0:T(8,128)(2,1)}, bf16[16,128,128]{2,1,0:T(8,128)(2,1)S(1)}, u32[]{:S(2)}) copy-start(bf16[16,128,128]{2,1,0:T(8,128)(2,1)S(1)} %collective-permute-done.5) | copy-start | bytes 1572868
  98.2 25.0 %collective-permute-start.7 = (bf16[16,128,128]{2,1,0:T(8,128)(2,1)S(1)}, bf16[16,128,128]{2,1,0:T(8,128)(2,1)}, u32[]{:S(2)}, u32[]{:S(2)}) collective-permute-start(bf16[16,128,128]{2,1,0:T(8,128)(2,1)S(1)} %collective-permute-done.5), channel_id=1, source_target_pairs={{0,120},{8,0},{16,8},{24,16},{32,24},{40,32},{48,40},{56,48},{64,5... | collective-permute-start | bytes 1572872 | tf_op jit(solution)/shard_map/ppermute | solution.py:104
  106.5 25.2 %collective-permute-start.8 = (bf16[16,128,128]{2,1,0:T(8,128)(2,1)}, bf16[16,128,128]{2,1,0:T(8,128)(2,1)}, u32[]{:S(2)}, u32[]{:S(2)}) collective-permute-start(bf16[16,128,128]{2,1,0:T(8,128)(2,1)} %collective-permute-done.6), channel_id=1, source_target_pairs={{0,8},{8,16},{16,24},{24,32},{32,40},{40,48},{48,56},{56,64},{64,7... | collective-permute-start | bytes 1572872 | tf_op jit(solution)/shard_map/ppermute | solution.py:96
  123.2 17.5 %collective-permute-start.9 = (bf16[16,128,128]{2,1,0:T(8,128)(2,1)}, bf16[16,128,128]{2,1,0:T(8,128)(2,1)}, u32[]{:S(2)}, u32[]{:S(2)}) collective-permute-start(bf16[16,128,128]{2,1,0:T(8,128)(2,1)} %collective-permute-done.7), channel_id=1, source_target_pairs={{0,120},{8,0},{16,8},{24,16},{32,24},{40,32},{48,40},{56,48},{64,5... | collective-permute-start | bytes 1572872 | tf_op jit(solution)/shard_map/ppermute | solution.py:104
  131.7 14.9 %collective-permute-start.10 = (bf16[16,128,128]{2,1,0:T(8,128)(2,1)}, bf16[16,128,128]{2,1,0:T(8,128)(2,1)S(1)}, u32[]{:S(2)}, u32[]{:S(2)}) collective-permute-start(bf16[16,128,128]{2,1,0:T(8,128)(2,1)} %collective-permute-done.8), channel_id=1, source_target_pairs={{0,8},{8,16},{16,24},{24,32},{32,40},{40,48},{48,56},{56,64},{64,7... | collective-permute-start | bytes 1572872 | tf_op jit(solution)/shard_map/ppermute | solution.py:96
  131.7 14.5 %collective-permute-start.1 = (bf16[7,128,128]{2,1,0:T(8,128)(2,1)S(1)}, bf16[7,128,128]{2,1,0:T(8,128)(2,1)S(1)}, u32[]{:S(2)}, u32[]{:S(2)}) collective-permute-start(bf16[7,128,128]{2,1,0:T(8,128)(2,1)S(1)} %slice.33), channel_id=1, source_target_pairs={{0,8},{8,16},{16,24},{24,32},{32,40},{40,48},{48,56},{56,64},{64,7... | collective-permute-start | bytes 688136 | tf_op jit(solution)/shard_map/ppermute | solution.py:15
  133.1 18.1 %collective-permute-start = (bf16[7,128,128]{2,1,0:T(8,128)(2,1)S(1)}, bf16[7,128,128]{2,1,0:T(8,128)(2,1)S(1)}, u32[]{:S(2)}, u32[]{:S(2)}) collective-permute-start(bf16[7,128,128]{2,1,0:T(8,128)(2,1)S(1)} %slice.32), channel_id=1, source_target_pairs={{0,8},{8,16},{16,24},{24,32},{32,40},{40,48},{48,56},{56,64},{64,7... | collective-permute-start | bytes 688136 | tf_op jit(solution)/shard_map/ppermute | solution.py:15
  140.7 14.0 %collective-permute-start.11 = (bf16[16,128,128]{2,1,0:T(8,128)(2,1)}, bf16[16,128,128]{2,1,0:T(8,128)(2,1)S(1)}, u32[]{:S(2)}, u32[]{:S(2)}) collective-permute-start(bf16[16,128,128]{2,1,0:T(8,128)(2,1)} %collective-permute-done.9), channel_id=1, source_target_pairs={{0,120},{8,0},{16,8},{24,16},{32,24},{40,32},{48,40},{56,48},{64,5... | collective-permute-start | bytes 1572872 | tf_op jit(solution)/shard_map/ppermute | solution.py:104
  146.3 13.7 %copy-start.4 = (bf16[16,128,128]{2,1,0:T(8,128)(2,1)S(1)}, bf16[16,128,128]{2,1,0:T(8,128)(2,1)}, u32[]{:S(2)}) copy-start(bf16[16,128,128]{2,1,0:T(8,128)(2,1)} %copy-done.3) | copy-start | bytes 1572868
  146.6 15.8 %collective-permute-start.12 = (bf16[16,128,128]{2,1,0:T(8,128)(2,1)S(1)}, bf16[16,128,128]{2,1,0:T(8,128)(2,1)S(1)}, u32[]{:S(2)}, u32[]{:S(2)}) collective-permute-start(bf16[16,128,128]{2,1,0:T(8,128)(2,1)S(1)} %collective-permute-done.10), channel_id=1, source_target_pairs={{0,8},{8,16},{16,24},{24,32},{32,40},{40,48},{48,56},{56,64},{64,7... | collective-permute-start | bytes 1572872 | tf_op jit(solution)/shard_map/ppermute | solution.py:96
  154.7 17.5 %collective-permute-start.13 = (bf16[16,128,128]{2,1,0:T(8,128)(2,1)S(1)}, bf16[16,128,128]{2,1,0:T(8,128)(2,1)S(1)}, u32[]{:S(2)}, u32[]{:S(2)}) collective-permute-start(bf16[16,128,128]{2,1,0:T(8,128)(2,1)S(1)} %collective-permute-done.11), channel_id=1, source_target_pairs={{0,120},{8,0},{16,8},{24,16},{32,24},{40,32},{48,40},{56,48},{64,5... | collective-permute-start | bytes 1572872 | tf_op jit(solution)/shard_map/ppermute | solution.py:104
  162.4 14.1 %collective-permute-start.14 = (bf16[16,128,128]{2,1,0:T(8,128)(2,1)S(1)}, bf16[16,128,128]{2,1,0:T(8,128)(2,1)S(1)}, u32[]{:S(2)}, u32[]{:S(2)}) collective-permute-start(bf16[16,128,128]{2,1,0:T(8,128)(2,1)S(1)} %collective-permute-done.12), channel_id=1, source_target_pairs={{0,8},{8,16},{16,24},{24,32},{32,40},{40,48},{48,56},{56,64},{64,7... | collective-permute-start | bytes 1572872 | tf_op jit(solution)/shard_map/ppermute | solution.py:96
  172.2 12.9 %collective-permute-start.15 = (bf16[16,128,128]{2,1,0:T(8,128)(2,1)S(1)}, bf16[16,128,128]{2,1,0:T(8,128)(2,1)S(1)}, u32[]{:S(2)}, u32[]{:S(2)}) collective-permute-start(bf16[16,128,128]{2,1,0:T(8,128)(2,1)S(1)} %collective-permute-done.13), channel_id=1, source_target_pairs={{0,120},{8,0},{16,8},{24,16},{32,24},{40,32},{48,40},{56,48},{64,5... | collective-permute-start | bytes 1572872 | tf_op jit(solution)/shard_map/ppermute | solution.py:104
  176.5 13.2 %collective-permute-start.16 = (bf16[16,128,128]{2,1,0:T(8,128)(2,1)S(1)}, bf16[16,128,128]{2,1,0:T(8,128)(2,1)S(1)}, u32[]{:S(2)}, u32[]{:S(2)}) collective-permute-start(bf16[16,128,128]{2,1,0:T(8,128)(2,1)S(1)} %collective-permute-done.14), channel_id=1, source_target_pairs={{0,8},{8,16},{16,24},{24,32},{32,40},{40,48},{48,56},{56,64},{64,7... | collective-permute-start | bytes 1572872 | tf_op jit(solution)/shard_map/ppermute | solution.py:96
  531.1 12.9 %copy-start.1 = (bf16[256,1024]{1,0:T(8,128)(2,1)S(1)}, bf16[256,1024]{1,0:T(8,128)(2,1)}, u32[]{:S(2)}) copy-start(bf16[256,1024]{1,0:T(8,128)(2,1)} %param.12) | copy-start | bytes 1572868
Sparse Core Ops, SparseCore 0:
  22.8 107.1 all-gather.1
